TPU v7x, 256 devices: a whole 4x4x8 slice. The times are simulated.
256 devices in a mesh: req: 128 (over z, y, x), tensor: 2 (over core).
Axes of the slice: x: 4, y: 4, z: 8, core: 2. Of those that a mesh axis runs over, the one named last changes fastest.
Arguments:
- patches: bfloat16 [256, 256, 1280], P('req'), may hold values from -6 to 6
- grids: int32 [256, 2], replicated, may hold values from 2 to 16, as said below
- place: int32 [256], replicated, may hold values from 0 to 255, as said below
- text_tokens: bfloat16 [128, 384, 1280], P('req'), may hold values from -6 to 6
- encoder_attend_in: bfloat16 [1280, 3, 1280], P(None, None, 'tensor'), may hold values from -0.15625 to 0.15625
- encoder_attend_out: bfloat16 [1280, 1280], P('tensor'), may hold values from -0.15625 to 0.15625
- encoder_expand: bfloat16 [1280, 5120], P(None, 'tensor'), may hold values from -0.15625 to 0.15625
- encoder_contract: bfloat16 [5120, 1280], P('tensor'), may hold values from -0.078125 to 0.078125
- encoder_gain_first: float32 [1280], replicated, may hold values from 0.25 to 1.75
- encoder_gain_second: float32 [1280], replicated, may hold values from 0.25 to 1.75
- merge_weight: bfloat16 [5120, 1280], P(None, 'tensor'), may hold values from -0.078125 to 0.078125
- decoder_attend_in: bfloat16 [1280, 3, 1280], P(None, None, 'tensor'), may hold values from -0.15625 to 0.15625
- decoder_attend_out: bfloat16 [1280, 1280], P('tensor'), may hold values from -0.15625 to 0.15625
- decoder_expand: bfloat16 [1280, 5120], P(None, 'tensor'), may hold values from -0.15625 to 0.15625
- decoder_contract: bfloat16 [5120, 1280], P('tensor'), may hold values from -0.078125 to 0.078125
- decoder_gain_first: float32 [1280], replicated, may hold values from 0.25 to 1.75
- decoder_gain_second: float32 [1280], replicated, may hold values from 0.25 to 1.75
Outputs:
- decoded: bfloat16 [128, 512, 1280], P('req')
Inputs may be any that keep to these rules, and one draw needn't show every extreme that they name: `grids`: both entries are even; image 0 always has the full 16 x 16 grid. A permutation: image i's merged tokens go to request place[i] // 2, image slot place[i] % 2. The request index, taken bitwise exclusive-or with i // 2, depends on i % 2 only: it is 1 when i % 2 = 0 and 64 when i % 2 = 1.
All inputs are finite; a program needn't handle non-finite values.
Results may differ from a plain program's by a relative error of at most 0.015.
Values may be sent and summed in bfloat16 or wider, within the bound.
No kernel may reach another device: no remote copies, remote signals or barrier semaphores. Data moves between devices by JAX's collectives and lax.ppermute only.
A program may use at most 192 MiB of HBM per device.

v0:
```python
import jax
import jax.numpy as jnp
from jax import lax
from jax.sharding import PartitionSpec as P

HEAD_DIM = 80
GRID = 16


def normalize(values, gain):
    center = values - jnp.mean(values, axis=-1, keepdims=True)
    spread = jnp.mean(center * center, axis=-1, keepdims=True)
    return center * lax.rsqrt(spread + 1e-06) * gain


def attend(normed, allowed, attend_in, attend_out):
    batch, length, width = normed.shape
    projected = jnp.dot(
        normed, attend_in.reshape(width, -1), preferred_element_type=jnp.float32
    ).astype(jnp.bfloat16)
    projected = projected.reshape(batch, length, 3, -1, HEAD_DIM)
    queries = projected[:, :, 0]
    key_rows = projected[:, :, 1]
    value_rows = projected[:, :, 2]
    scores = jnp.einsum(
        "bqhd,bkhd->bhqk", queries, key_rows, preferred_element_type=jnp.float32
    ) * HEAD_DIM ** (-0.5)
    scores = jnp.where(allowed[:, None], scores, jnp.float32(-1e30))
    probs = jax.nn.softmax(scores, axis=-1).astype(jnp.bfloat16)
    mixed = jnp.einsum(
        "bhqk,bkhd->bqhd", probs, value_rows, preferred_element_type=jnp.float32
    ).astype(jnp.bfloat16)
    return jnp.dot(mixed.reshape(batch, length, -1), attend_out, preferred_element_type=jnp.float32)


def layer(inputs, allowed, attend_in, attend_out, expand, contract, gain_first, gain_second):
    widened = inputs.astype(jnp.float32)
    first = normalize(widened, gain_first).astype(jnp.bfloat16)
    attended = attend(first, allowed, attend_in, attend_out)
    residual = widened + lax.psum(attended.astype(jnp.bfloat16), "tensor").astype(jnp.float32)
    second = normalize(residual, gain_second).astype(jnp.bfloat16)
    hidden = jax.nn.gelu(
        jnp.dot(second, expand, preferred_element_type=jnp.float32), approximate=False
    ).astype(jnp.bfloat16)
    partial_out = jnp.dot(hidden, contract, preferred_element_type=jnp.float32)
    return (
        residual + lax.psum(partial_out.astype(jnp.bfloat16), "tensor").astype(jnp.float32)
    ).astype(jnp.bfloat16)


def on_device(
    patches,
    grids,
    place,
    text_tokens,
    encoder_attend_in,
    encoder_attend_out,
    encoder_expand,
    encoder_contract,
    encoder_gain_first,
    encoder_gain_second,
    merge_weight,
    decoder_attend_in,
    decoder_attend_out,
    decoder_expand,
    decoder_contract,
    decoder_gain_first,
    decoder_gain_second,
):
    device = lax.axis_index("req")
    images_here, cell_count, width = patches.shape
    side = GRID
    half = side // 2
    slot_count = half * half
    local_grids = lax.dynamic_slice_in_dim(grids, device * images_here, images_here, 0)
    cells = jnp.arange(cell_count)
    cell_valid = ((cells // side)[None, :] < local_grids[:, 0:1]) & (
        (cells % side)[None, :] < local_grids[:, 1:2]
    )
    image_allowed = jnp.broadcast_to(cell_valid[:, None, :], (images_here, cell_count, cell_count))
    encoded = layer(
        patches,
        image_allowed,
        encoder_attend_in,
        encoder_attend_out,
        encoder_expand,
        encoder_contract,
        encoder_gain_first,
        encoder_gain_second,
    )
    blocks = (
        encoded.reshape(images_here, half, 2, half, 2, width)
        .transpose(0, 1, 3, 2, 4, 5)
        .reshape(images_here * slot_count, 4 * width)
    )
    merged = jnp.dot(blocks, merge_weight, preferred_element_type=jnp.float32).astype(jnp.bfloat16)
    merged = merged.reshape(images_here, slot_count, -1)
    wanted = device * images_here + jnp.arange(images_here)
    matches = place[None, :] == wanted[:, None]
    everything = lax.all_gather(merged, "req", axis=0, tiled=True)
    arranged = jnp.einsum(
        "qg,gmc->qmc", matches.astype(jnp.bfloat16), everything, preferred_element_type=jnp.float32
    ).astype(jnp.bfloat16)
    slot_grids = jnp.sum(matches.astype(jnp.int32)[:, :, None] * grids[None, :, :], axis=1)
    slots = jnp.arange(slot_count)
    merged_valid = ((2 * (slots // half))[None, :] < slot_grids[:, 0:1]) & (
        (2 * (slots % half))[None, :] < slot_grids[:, 1:2]
    )
    image_rows = lax.all_gather(
        arranged.reshape(images_here * slot_count, -1), "tensor", axis=1, tiled=True
    )
    prompt = jnp.concatenate([image_rows, text_tokens[0]], axis=0)[None]
    text_count = text_tokens.shape[1]
    prompt_valid = jnp.concatenate(
        [merged_valid.reshape(-1), jnp.ones((text_count,), bool)], axis=0
    )
    length = prompt.shape[1]
    positions = jnp.arange(length)
    prompt_allowed = (prompt_valid[None, :] & (positions[None, :] <= positions[:, None]))[None]
    decoded = layer(
        prompt,
        prompt_allowed,
        decoder_attend_in,
        decoder_attend_out,
        decoder_expand,
        decoder_contract,
        decoder_gain_first,
        decoder_gain_second,
    )
    return jnp.where(prompt_valid[None, :, None], decoded, jnp.zeros_like(decoded))


def solution(mesh):
    placed = (
        P("req", None, None),
        P(),
        P(),
        P("req", None, None),
        P(None, None, "tensor"),
        P("tensor", None),
        P(None, "tensor"),
        P("tensor", None),
        P(),
        P(),
        P(None, "tensor"),
        P(None, None, "tensor"),
        P("tensor", None),
        P(None, "tensor"),
        P("tensor", None),
        P(),
        P(),
    )
    return jax.shard_map(
        on_device, mesh=mesh, in_specs=placed, out_specs=P("req", None, None), check_vma=False
    )
```

profile of v0, /device:TPU:1, one launch (start us, length us, event | category | flops | bytes accessed | tf_op | source)
XLA Modules:
  0.0 464.2 jit_solution(3344915803614442546)
XLA Ops:
  7.4 1.6 convert_reduce_fusion.1
  9.0 1.8 fusion.41
  10.8 8.3 %copy.73 = bf16[1280,3,640]{0,2,1:T(8,128)(2,1)} copy(bf16[1280,3,640]{2,0,1:T(8,128)(2,1)} %param.21) | data formatting | bytes 9830400 | tf_op args[4]
  19.1 6.7 %convolution_convert_fusion.4 = bf16[2,256,1920]{2,1,0:T(8,128)(2,1)} fusion(bf16[1280,1920,1]{0,1,2:T(8,128)(2,1)} %bitcast.112, bf16[2,256,1280]{2,1,0:T(8,128)(2,1)S(1)} %copy-done.2, f32[1280]{0:T(1024)S(1)} %copy-done.9, f32[2,256]{1,0:T(2,128)S(1)} %add_rsqrt_fusion.3, f32[2,256]{1,0:T(2,128)S(1)} %broadcast_multiply_fusion.3), kind=kOutput, calls=%fused_computation.74 | convolution fusion | flops 2520842240 | bytes 8201216 | tf_op jit(solution)/shard_map/dot_general | solution.py:18
  25.8 4.0 copy.75
  29.8 2.0 fusion.153
  33.5 1.6 fusion.114
  35.1 2.3 convolution_convert_fusion.1
  37.6 35.2 %all-reduce.6.cloned.1.call-done = bf16[2,256,1280]{2,1,0:T(8,128)(2,1)} async-done(((bf16[2,256,1280]{2,1,0:T(8,128)(2,1)}), bf16[2,256,1280]{2,1,0:T(8,128)(2,1)}) %all-reduce.6.cloned.1.call-update) | async-done | bytes 1310736 | tf_op jit(solution)/shard_map/psum | solution.py:40
  72.8 1.8 fusion.107
  74.7 2.1 multiply_reduce_fusion.1
  76.8 8.1 %fusion.144 = (u8[256,2560]{1,0:T(8,128)(4,1)S(1)}, u8[256,2560]{1,0:T(8,128)(4,1)S(1)}, f32[2,256,2560]{2,1,0:T(8,128)S(1)}) fusion(bf16[1280,2560]{1,0:T(8,128)(2,1)} %param.23, bf16[2,256,1280]{2,1,0:T(8,128)(2,1)S(1)} %copy-done.4, bf16[2,256,1280]{2,1,0:T(8,128)(2,1)S(1)} %copy-done.2, f32[1280]{0:T(1024)S(1)} %copy-done.10, ...), kind=kOutput, calls=%fused_computation.179 | convolution fusion | flops 3375759360 | bytes 15737856 | tf_op jit(solution)/shard_map/dot_general | solution.py:43
  84.9 16.2 %fusion.35 = bf16[2,256,1280]{2,1,0:T(8,128)(2,1)} fusion(bf16[2560,1280]{1,0:T(8,128)(2,1)S(1)} %bitcast.118, f32[2,256,2560]{2,1,0:T(8,128)S(1)} %get-tuple-element.13, u8[256,2560]{1,0:T(8,128)(4,1)S(1)} %get-tuple-element.6, u8[256,2560]{1,0:T(8,128)(4,1)S(1)} %get-tuple-element.5), kind=kOutput, calls=%fused_computation.71 | convolution fusion | flops 3447848960 | bytes 14417920 | tf_op jit(solution)/shard_map/dot_general | solution.py:45
  101.2 32.2 %all-reduce.8.cloned.1.call-done = bf16[2,256,1280]{2,1,0:T(8,128)(2,1)} async-done(((bf16[2,256,1280]{2,1,0:T(8,128)(2,1)}), bf16[2,256,1280]{2,1,0:T(8,128)(2,1)}) %all-reduce.8.cloned.1.call-update) | async-done | bytes 1310736 | tf_op jit(solution)/shard_map/psum | solution.py:47
  133.4 2.8 add_convert_fusion.1
  136.2 3.1 reshape.449
  141.3 4.7 %convolution_convert_fusion.5 = bf16[128,640]{1,0:T(8,128)(2,1)} fusion(bf16[128,5120]{1,0:T(8,128)(2,1)S(1)} %reshape.450, bf16[5120,640]{1,0:T(8,128)(2,1)} %param.27), kind=kOutput, calls=%fused_computation.181 | convolution fusion | flops 838942720 | bytes 8028160 | tf_op jit(solution)/shard_map/dot_general | solution.py:96
  146.1 8.6 %copy.84 = bf16[1280,3,640]{0,2,1:T(8,128)(2,1)} copy(bf16[1280,3,640]{2,0,1:T(8,128)(2,1)} %param.28) | data formatting | bytes 9830400 | tf_op args[11]
  155.6 155.3 %all-gather.2.cloned.1.call-done = bf16[256,64,640]{2,1,0:T(8,128)(2,1)} async-done(((bf16[2,64,640]{2,1,0:T(8,128)(2,1)}), bf16[256,64,640]{2,1,0:T(8,128)(2,1)}) %all-gather.2.cloned.1.call-update) | async-done | bytes 20971536 | tf_op jit(solution)/shard_map/all_gather | solution.py:100
  310.9 29.1 %fusion.145 = bf16[2,64,640]{2,0,1:T(2,128)(2,1)S(1)} fusion(bf16[256,64,640]{2,1,0:T(8,128)(2,1)} %all-gather.2.cloned.1.call-done, s32[256]{0:T(256)S(1)} %copy-done.7, s32[2]{0:T(128)S(1)} %iota_add_fusion), kind=kOutput, calls=%fused_computation.180 | convolution fusion | flops 42025472 | bytes 21136392 | tf_op jit(solution)/shard_map/qg,gmc->qmc/dot_general | solution.py:101
  340.0 2.7 all_gather.7
  343.5 4.6 convolution_convert_fusion.3
  348.1 4.0 copy.85
  352.1 7.7 %fusion.228 = (f32[8,512]{1,0:T(8,128)S(1)}, f32[8,512,512]{1,2,0:T(8,128)}) fusion(pred[512,512]{0,1:T(8,128)(4,1)S(1)} %fusion.148, bf16[1,512,3,8,80]{1,4,3,2,0:T(8,128)(2,1)} %bitcast.113), kind=kOutput, calls=%fused_computation.297 | convolution fusion | flops 343933440 | bytes 9977856 | tf_op jit(solution)/shard_map/sub | solution.py:29
  359.7 4.6 fusion.115
  364.3 2.3 fusion.39
  366.9 28.2 %all-reduce.10.cloned.1.call-done = bf16[1,512,1280]{2,1,0:T(8,128)(2,1)} async-done(((bf16[1,512,1280]{2,1,0:T(8,128)(2,1)}), bf16[1,512,1280]{2,1,0:T(8,128)(2,1)}) %all-reduce.10.cloned.1.call-update) | async-done | bytes 1310736 | tf_op jit(solution)/shard_map/psum | solution.py:40
  395.1 1.7 fusion.108
  396.8 1.9 multiply_reduce_fusion
  398.7 22.9 %fusion.38 = bf16[1,512,1280]{2,1,0:T(8,128)(2,1)} fusion(bf16[2560,1280]{1,0:T(8,128)(2,1)} %param.31, bf16[1280,2560]{1,0:T(8,128)(2,1)} %param.30, bf16[1,512,1280]{2,1,0:T(8,128)(2,1)} %all-reduce.10.cloned.1.call-done, f32[1280]{0:T(1024)S(1)} %copy-done.12, f32[512]{0:T(512)S(1)} %add_rsqrt_fusion, f32[512]{0:T(512)S(1)} %broadcast_multiply_fusion, ...), kind=kOutput, calls=%fused_computation.75 | convolution fusion | flops 6803292160 | bytes 17048576 | tf_op jit(solution)/shard_map/dot_general | solution.py:45
  421.6 32.2 %all-reduce.12.cloned.1.call-done = bf16[1,512,1280]{2,1,0:T(8,128)(2,1)} async-done(((bf16[1,512,1280]{2,1,0:T(8,128)(2,1)}), bf16[1,512,1280]{2,1,0:T(8,128)(2,1)}) %all-reduce.12.cloned.1.call-update) | async-done | bytes 1310736 | tf_op jit(solution)/shard_map/psum | solution.py:47
  453.9 3.3 fusion.123
  (68 shorter events, 6.8 us)
Async XLA Ops:
  6.5 28.5 %copy-start = (bf16[640,1280]{1,0:T(8,128)(2,1)S(1)}, bf16[640,1280]{1,0:T(8,128)(2,1)}, u32[]{:S(2)}) copy-start(bf16[640,1280]{1,0:T(8,128)(2,1)} %param.22) | copy-start | bytes 4915204
  6.5 66.3 %all-reduce.6.cloned.1.call-start = ((), (), s32[]{:S(2)}) async-start(), calls=%async_computation | async-start | bytes 2621440 | tf_op jit(solution)/shard_map/psum | solution.py:40
  10.8 8.3 %copy-start.2 = (bf16[2,256,1280]{2,1,0:T(8,128)(2,1)S(1)}, bf16[2,256,1280]{2,1,0:T(8,128)(2,1)}, u32[]{:S(2)}) copy-start(bf16[2,256,1280]{2,1,0:T(8,128)(2,1)} %param.17) | copy-start | bytes 3932164
  10.8 8.3 %copy-start.9 = (f32[1280]{0:T(1024)S(1)}, f32[1280]{0:T(1024)}, u32[]{:S(2)}) copy-start(f32[1280]{0:T(1024)} %param.25) | copy-start | bytes 15364
  35.1 41.7 %copy-start.10 = (f32[1280]{0:T(1024)S(1)}, f32[1280]{0:T(1024)}, u32[]{:S(2)}) copy-start(f32[1280]{0:T(1024)} %param.26) | copy-start | bytes 15364
  37.4 96.0 %all-reduce.8.cloned.1.call-start = ((), (), s32[]{:S(2)}) async-start(), calls=%async_computation.1 | async-start | bytes 2621440 | tf_op jit(solution)/shard_map/psum | solution.py:47
  72.8 3.9 copy-start.4
  74.7 10.2 %slice-start = ((s8[6553600]{0:T(1024)(128)(4,1)}), s8[4194304]{0:T(1024)(128)(4,1)S(1)}, s32[]{:S(2)}) async-start(s8[6553600]{0:T(1024)(128)(4,1)} %bitcast.117), calls=%async_computation.5 | async-start | bytes 8388608
  76.8 8.1 %slice-start.1 = ((s8[6553600]{0:T(1024)(128)(4,1)}), s8[2359296]{0:T(1024)(128)(4,1)S(1)}, s32[]{:S(2)}) async-start(s8[6553600]{0:T(1024)(128)(4,1)} %bitcast.117), calls=%async_computation.6 | async-start | bytes 4718592
  101.1 209.7 %all-gather.2.cloned.1.call-start = ((), (), s32[]{:S(2)}) async-start(), calls=%async_computation.2 | async-start | bytes 21135360 | tf_op jit(solution)/shard_map/all_gather | solution.py:100
  146.0 8.8 %copy-start.7 = (s32[256]{0:T(256)S(1)}, s32[256]{0:T(256)}, u32[]{:S(2)}) copy-start(s32[256]{0:T(256)} %param.19) | copy-start | bytes 3076
  146.1 8.8 %copy-start.6 = (s32[256,2]{0,1:T(2,128)S(1)}, s32[256,2]{0,1:T(2,128)}, u32[]{:S(2)}) copy-start(s32[256,2]{0,1:T(2,128)} %param.18) | copy-start | bytes 6148
  146.1 249.0 %all-reduce.10.cloned.1.call-start = ((), (), s32[]{:S(2)}) async-start(), calls=%async_computation.3 | async-start | bytes 2621440 | tf_op jit(solution)/shard_map/psum | solution.py:40
  155.5 187.2 %copy-start.3 = (bf16[1,384,1280]{2,1,0:T(8,128)(2,1)S(1)}, bf16[1,384,1280]{2,1,0:T(8,128)(2,1)}, u32[]{:S(2)}) copy-start(bf16[1,384,1280]{2,1,0:T(8,128)(2,1)} %param.20) | copy-start | bytes 2949124
  155.5 187.9 %copy-start.11 = (f32[1280]{0:T(1024)S(1)}, f32[1280]{0:T(1024)}, u32[]{:S(2)}) copy-start(f32[1280]{0:T(1024)} %param.32) | copy-start | bytes 15364
  310.9 32.6 %copy-start.5 = (bf16[1280,3,640]{0,2,1:T(8,128)(2,1)S(1)}, bf16[1280,3,640]{0,2,1:T(8,128)(2,1)}, u32[]{:S(2)}) copy-start(bf16[1280,3,640]{0,2,1:T(8,128)(2,1)} %copy.84) | copy-start | bytes 14745604
  359.7 4.6 copy-start.8
  366.6 32.1 %copy-start.12 = (f32[1280]{0:T(1024)S(1)}, f32[1280]{0:T(1024)}, u32[]{:S(2)}) copy-start(f32[1280]{0:T(1024)} %param.33) | copy-start | bytes 15364
  366.6 87.2 %all-reduce.12.cloned.1.call-start = ((), (), s32[]{:S(2)}) async-start(), calls=%async_computation.4 | async-start | bytes 2621440 | tf_op jit(solution)/shard_map/psum | solution.py:47
  398.7 58.5 %copy-start.1 = (bf16[640,1280]{1,0:T(8,128)(2,1)S(1)}, bf16[640,1280]{1,0:T(8,128)(2,1)}, u32[]{:S(2)}) copy-start(bf16[640,1280]{1,0:T(8,128)(2,1)} %param.22) | copy-start | bytes 4915204
Sparse Core Ops, SparseCore 0:
  37.5 35.3 all-reduce.5
  101.3 32.0 all-reduce.7
  146.2 164.6 all-gather.1
  366.7 28.2 all-reduce.9
  421.7 32.0 all-reduce.11
where the time goes:
time: 470 us; the launch traced here: 464 us
  waiting for transfers between devices  283 us (60%)
  matrix products  113 us (24%)
  local copies, waits for them, and re-layouts  31.2 us (7%)
  other arithmetic  19.9 us (4%)
  between operations  13.9 us (3%)
    all_gather x1, waiting for transfers between devices, on_device(): everything = lax.all_gather(merged, 'req', axis=0, tiled=True)  155 us
    psum x2, waiting for transfers between devices, layer(): lax.psum(partial_out.astype(jnp.bfloat16), 'tensor').astype(jnp.float32)  64.4 us
    psum x2, waiting for transfers between devices, layer(): lax.psum(attended.astype(jnp.bfloat16), 'tensor').astype(jnp.float32)  63.4 us
    dot_general x2, matrix products, layer(): partial_out = jnp.dot(hidden, contract, preferred_element_type=jnp.float32)  39.1 us
    dot_general x1, matrix products, on_device(): jnp.einsum('qg,gmc->qmc', matches.astype(jnp.bfloat16), everything, prefe...  29.1 us
    unnamed x32, local copies, waits for them, and re-layouts  17 us
    dot_general x2, matrix products, attend(): jnp.dot(normed, attend_in.reshape(width, -1), preferred_element_type=jnp....  11.3 us
  transfers between devices with their start and end apart: 5, of which 5 were waited for; matrix products, arithmetic and copies ran while one was open for 2% of the time, Pallas kernels for 0%

commit v1 on v0

--- a/solution.py
+++ b/solution.py
@@ -37,7 +37,9 @@
     widened = inputs.astype(jnp.float32)
     first = normalize(widened, gain_first).astype(jnp.bfloat16)
     attended = attend(first, allowed, attend_in, attend_out)
-    residual = widened + lax.psum(attended.astype(jnp.bfloat16), "tensor").astype(jnp.float32)
+    residual = widened + jnp.sum(
+        lax.all_gather(attended.astype(jnp.bfloat16), "tensor"), axis=0
+    ).astype(jnp.float32)
     second = normalize(residual, gain_second).astype(jnp.bfloat16)
     hidden = jax.nn.gelu(
         jnp.dot(second, expand, preferred_element_type=jnp.float32), approximate=False

time: 470 us -> 442 us (0.940)
  waiting for transfers between devices: 283 us -> 255 us
    psum x2 -> x0, waiting for transfers between devices: 63.4 us -> none  [layer(): lax.psum(attended.astype(jnp.bfloat16), 'tensor').astype(jnp.float32)]
    all_gather x0 -> x2, waiting for transfers between devices: none -> 35 us  [layer(): lax.all_gather(attended.astype(jnp.bfloat16), 'tensor')]
    reduce_sum x0 -> x2, other arithmetic: none -> 5.53 us  [layer(): jnp.sum(lax.all_gather(attended.astype(jnp.bfloat16), 'tensor'), axis=0)]
where the time goes in v1:
time: 442 us; the launch traced here: 437 us
  waiting for transfers between devices  255 us (58%)
  matrix products  113 us (26%)
  local copies, waits for them, and re-layouts  31.5 us (7%)
  other arithmetic  19.9 us (5%)
  between operations  13.7 us (3%)
    all_gather x1, waiting for transfers between devices, on_device(): everything = lax.all_gather(merged, 'req', axis=0, tiled=True)  156 us
    psum x2, waiting for transfers between devices, layer(): lax.psum(partial_out.astype(jnp.bfloat16), 'tensor').astype(jnp.float32)  64.4 us
    dot_general x2, matrix products, layer(): partial_out = jnp.dot(hidden, contract, preferred_element_type=jnp.float32)  39.1 us
    all_gather x2, waiting for transfers between devices, layer(): lax.all_gather(attended.astype(jnp.bfloat16), 'tensor')  35 us
    dot_general x1, matrix products, on_device(): jnp.einsum('qg,gmc->qmc', matches.astype(jnp.bfloat16), everything, prefe...  29.3 us
    unnamed x32, local copies, waits for them, and re-layouts  17.4 us
    dot_general x2, matrix products, attend(): jnp.dot(normed, attend_in.reshape(width, -1), preferred_element_type=jnp....  11.3 us
  transfers between devices with their start and end apart: 5, of which 5 were waited for; matrix products, arithmetic and copies ran while one was open for 2% of the time, Pallas kernels for 0%

profile of v1, /device:TPU:1, one launch (start us, length us, event | category | flops | bytes accessed | tf_op | source)
XLA Modules:
  0.0 436.9 jit_solution(13043119547038196597)
XLA Ops:
  7.4 1.6 convert_reduce_fusion.1
  9.0 1.8 fusion.40
  10.8 8.3 %copy.73 = bf16[1280,3,640]{0,2,1:T(8,128)(2,1)} copy(bf16[1280,3,640]{2,0,1:T(8,128)(2,1)} %param.21) | data formatting | bytes 9830400 | tf_op args[4]
  19.1 6.7 %convolution_convert_fusion.4 = bf16[2,256,1920]{2,1,0:T(8,128)(2,1)} fusion(bf16[1280,1920,1]{0,1,2:T(8,128)(2,1)} %bitcast.115, bf16[2,256,1280]{2,1,0:T(8,128)(2,1)S(1)} %copy-done.2, f32[1280]{0:T(1024)S(1)} %copy-done.9, f32[2,256]{1,0:T(2,128)S(1)} %add_rsqrt_fusion.3, f32[2,256]{1,0:T(2,128)S(1)} %broadcast_multiply_fusion.3), kind=kOutput, calls=%fused_computation.77 | convolution fusion | flops 2520842240 | bytes 8201216 | tf_op jit(solution)/shard_map/dot_general | solution.py:18
  25.8 4.0 copy.75
  29.8 2.0 fusion.147
  31.9 1.5 fusion.223
  33.5 1.6 fusion.116
  35.1 2.3 convolution_convert_fusion.1
  37.9 20.8 %all-gather.8.cloned.1.call-done = bf16[4,256,1280]{2,1,0:T(8,128)(2,1)} async-done(((bf16[2,256,1280]{2,1,0:T(8,128)(2,1)}), bf16[4,256,1280]{2,1,0:T(8,128)(2,1)}) %all-gather.8.cloned.1.call-update) | async-done | bytes 2621456 | tf_op jit(solution)/shard_map/all_gather | solution.py:41
  58.7 2.6 reduce_sum.127
  62.4 8.4 %fusion.138 = (u8[256,2560]{1,0:T(8,128)(4,1)S(1)}, u8[256,2560]{1,0:T(8,128)(4,1)S(1)}, f32[2,256,2560]{2,1,0:T(8,128)S(1)}) fusion(bf16[1280,2560]{1,0:T(8,128)(2,1)} %param.23, bf16[2,256,1280]{2,1,0:T(8,128)(2,1)S(1)} %reduce_sum.127, bf16[2,256,1280]{2,1,0:T(8,128)(2,1)S(1)} %copy-done.2, f32[1280]{0:T(1024)S(1)} %copy-done.10, ...), kind=kOutput, calls=%fused_computation.180 | convolution fusion | flops 3375759360 | bytes 15737856 | tf_op jit(solution)/shard_map/dot_general | solution.py:45
  70.8 16.2 %fusion.35 = bf16[2,256,1280]{2,1,0:T(8,128)(2,1)} fusion(bf16[2560,1280]{1,0:T(8,128)(2,1)S(1)} %bitcast.123, f32[2,256,2560]{2,1,0:T(8,128)S(1)} %get-tuple-element.13, u8[256,2560]{1,0:T(8,128)(4,1)S(1)} %get-tuple-element.6, u8[256,2560]{1,0:T(8,128)(4,1)S(1)} %get-tuple-element.5), kind=kOutput, calls=%fused_computation.74 | convolution fusion | flops 3447848960 | bytes 14417920 | tf_op jit(solution)/shard_map/dot_general | solution.py:47
  87.1 32.2 %all-reduce.4.cloned.1.call-done = bf16[2,256,1280]{2,1,0:T(8,128)(2,1)} async-done(((bf16[2,256,1280]{2,1,0:T(8,128)(2,1)}), bf16[2,256,1280]{2,1,0:T(8,128)(2,1)}) %all-reduce.4.cloned.1.call-update) | async-done | bytes 1310736 | tf_op jit(solution)/shard_map/psum | solution.py:49
  119.3 2.8 add_convert_fusion.1
  122.1 3.1 reshape.553
  126.2 1.0 reshape.554
  127.2 4.7 %convolution_convert_fusion.5 = bf16[128,640]{1,0:T(8,128)(2,1)} fusion(bf16[128,5120]{1,0:T(8,128)(2,1)S(1)} %reshape.554, bf16[5120,640]{1,0:T(8,128)(2,1)} %param.27), kind=kOutput, calls=%fused_computation.182 | convolution fusion | flops 838942720 | bytes 8028160 | tf_op jit(solution)/shard_map/dot_general | solution.py:98
  132.0 8.4 %copy.84 = bf16[1280,3,640]{0,2,1:T(8,128)(2,1)} copy(bf16[1280,3,640]{2,0,1:T(8,128)(2,1)} %param.28) | data formatting | bytes 9830400 | tf_op args[11]
  141.2 155.6 %all-gather.6.cloned.1.call-done = bf16[256,64,640]{2,1,0:T(8,128)(2,1)} async-done(((bf16[2,64,640]{2,1,0:T(8,128)(2,1)}), bf16[256,64,640]{2,1,0:T(8,128)(2,1)}) %all-gather.6.cloned.1.call-update) | async-done | bytes 20971536 | tf_op jit(solution)/shard_map/all_gather | solution.py:102
  296.8 29.3 %fusion.139 = bf16[2,64,640]{2,0,1:T(2,128)(2,1)S(1)} fusion(bf16[256,64,640]{2,1,0:T(8,128)(2,1)} %all-gather.6.cloned.1.call-done, s32[256]{0:T(256)S(1)} %copy-done.7, s32[2]{0:T(128)S(1)} %iota_add_fusion), kind=kOutput, calls=%fused_computation.181 | convolution fusion | flops 42025472 | bytes 21136392 | tf_op jit(solution)/shard_map/qg,gmc->qmc/dot_general | solution.py:103
  326.1 2.7 all_gather.21
  329.6 4.6 %convolution_convert_fusion.3 = bf16[512,1920]{1,0:T(8,128)(2,1)} fusion(bf16[1280,1920]{0,1:T(8,128)(2,1)S(1)} %bitcast.114, f32[1280]{0:T(1024)S(1)} %copy-done.11, f32[512]{0:T(512)S(1)} %add_rsqrt_fusion.1, f32[512]{0:T(512)S(1)} %broadcast_multiply_fusion.1, bf16[384,1280]{1,0:T(8,128)(2,1)S(1)} %bitcast.104, bf16[128,1280]{1,0:T(8,128)(2,1)S(1)} %all_gather.21), kind=kOutput, calls=%fused_computation.76 | convolution fusion | flops 2522808320 | bytes 8201216 | tf_op jit(solution)/shard_map/dot_general | solution.py:18
  334.2 4.0 copy.85
  338.2 7.7 %fusion.224 = (f32[8,512]{1,0:T(8,128)S(1)}, f32[8,512,512]{1,2,0:T(8,128)}) fusion(pred[512,512]{0,1:T(8,128)(4,1)S(1)} %fusion.142, bf16[1,512,3,8,80]{1,4,3,2,0:T(8,128)(2,1)} %bitcast.118), kind=kOutput, calls=%fused_computation.299 | convolution fusion | flops 343933440 | bytes 9977856 | tf_op jit(solution)/shard_map/sub | solution.py:29
  345.9 4.6 %fusion.117 = bf16[8,80,512]{2,1,0:T(8,128)(2,1)S(1)} fusion(f32[8,512,512]{1,2,0:T(8,128)} %get-tuple-element.15, f32[8,512]{1,0:T(8,128)S(1)} %get-tuple-element.14, bf16[1,512,3,8,80]{1,4,3,2,0:T(8,128)(2,1)} %bitcast.119), kind=kOutput, calls=%fused_computation.161 | convolution fusion | flops 340066304 | bytes 9715712 | tf_op jit(solution)/shard_map/bhqk,bkhd->bqhd/dot_general | solution.py:30
  350.4 2.3 convolution_convert_fusion
  353.0 14.1 %all-gather.10.cloned.1.call-done = bf16[1024,1280]{1,0:T(8,128)(2,1)} async-done(((bf16[512,1280]{1,0:T(8,128)(2,1)}), bf16[1024,1280]{1,0:T(8,128)(2,1)}) %all-gather.10.cloned.1.call-update) | async-done | bytes 2621456 | tf_op jit(solution)/shard_map/all_gather | solution.py:41
  367.1 3.0 reduce.12
  371.7 22.9 %fusion.38 = bf16[1,512,1280]{2,1,0:T(8,128)(2,1)} fusion(bf16[2560,1280]{1,0:T(8,128)(2,1)} %param.31, bf16[1280,2560]{1,0:T(8,128)(2,1)} %param.30, bf16[512,1280]{1,0:T(8,128)(2,1)} %copy-done.4, f32[1280]{0:T(1024)S(1)} %copy-done.12, f32[512]{0:T(512)S(1)} %add_rsqrt_fusion, f32[512]{0:T(512)S(1)} %broadcast_multiply_fusion, ...), kind=kOutput, calls=%fused_computation.78 | convolution fusion | flops 6803292160 | bytes 17048576 | tf_op jit(solution)/shard_map/dot_general | solution.py:47
  394.6 32.2 %all-reduce.6.cloned.1.call-done = bf16[1,512,1280]{2,1,0:T(8,128)(2,1)} async-done(((bf16[1,512,1280]{2,1,0:T(8,128)(2,1)}), bf16[1,512,1280]{2,1,0:T(8,128)(2,1)}) %all-reduce.6.cloned.1.call-update) | async-done | bytes 1310736 | tf_op jit(solution)/shard_map/psum | solution.py:49
  426.8 3.3 fusion.119
  (70 shorter events, 7.1 us)
Async XLA Ops:
  6.5 28.5 %copy-start = (bf16[640,1280]{1,0:T(8,128)(2,1)S(1)}, bf16[640,1280]{1,0:T(8,128)(2,1)}, u32[]{:S(2)}) copy-start(bf16[640,1280]{1,0:T(8,128)(2,1)} %param.22) | copy-start | bytes 4915204
  6.5 52.2 %all-gather.8.cloned.1.call-start = ((), (), s32[]{:S(2)}) async-start(), calls=%async_computation.3 | async-start | bytes 3932160 | tf_op jit(solution)/shard_map/all_gather | solution.py:41
  10.8 8.3 %copy-start.2 = (bf16[2,256,1280]{2,1,0:T(8,128)(2,1)S(1)}, bf16[2,256,1280]{2,1,0:T(8,128)(2,1)}, u32[]{:S(2)}) copy-start(bf16[2,256,1280]{2,1,0:T(8,128)(2,1)} %param.17) | copy-start | bytes 3932164
  10.8 8.3 %copy-start.9 = (f32[1280]{0:T(1024)S(1)}, f32[1280]{0:T(1024)}, u32[]{:S(2)}) copy-start(f32[1280]{0:T(1024)} %param.25) | copy-start | bytes 15364
  37.4 25.0 %copy-start.10 = (f32[1280]{0:T(1024)S(1)}, f32[1280]{0:T(1024)}, u32[]{:S(2)}) copy-start(f32[1280]{0:T(1024)} %param.26) | copy-start | bytes 15364
  37.4 81.9 %all-reduce.4.cloned.1.call-start = ((), (), s32[]{:S(2)}) async-start(), calls=%async_computation | async-start | bytes 2621440 | tf_op jit(solution)/shard_map/psum | solution.py:49
  61.7 9.1 %slice-start = ((s8[6553600]{0:T(1024)(128)(4,1)}), s8[4194304]{0:T(1024)(128)(4,1)S(1)}, s32[]{:S(2)}) async-start(s8[6553600]{0:T(1024)(128)(4,1)} %bitcast.122), calls=%async_computation.5 | async-start | bytes 8388608
  62.4 8.4 %slice-start.1 = ((s8[6553600]{0:T(1024)(128)(4,1)}), s8[2359296]{0:T(1024)(128)(4,1)S(1)}, s32[]{:S(2)}) async-start(s8[6553600]{0:T(1024)(128)(4,1)} %bitcast.122), calls=%async_computation.6 | async-start | bytes 4718592
  87.0 209.7 %all-gather.6.cloned.1.call-start = ((), (), s32[]{:S(2)}) async-start(), calls=%async_computation.1 | async-start | bytes 21135360 | tf_op jit(solution)/shard_map/all_gather | solution.py:102
  131.9 8.5 %copy-start.7 = (s32[256]{0:T(256)S(1)}, s32[256]{0:T(256)}, u32[]{:S(2)}) copy-start(s32[256]{0:T(256)} %param.19) | copy-start | bytes 3076
  131.9 8.5 %copy-start.6 = (s32[256,2]{0,1:T(2,128)S(1)}, s32[256,2]{0,1:T(2,128)}, u32[]{:S(2)}) copy-start(s32[256,2]{0,1:T(2,128)} %param.18) | copy-start | bytes 6148
  132.0 235.1 %all-gather.10.cloned.1.call-start = ((), (), s32[]{:S(2)}) async-start(), calls=%async_computation.4 | async-start | bytes 3932160 | tf_op jit(solution)/shard_map/all_gather | solution.py:41
  141.1 187.7 %copy-start.3 = (bf16[1,384,1280]{2,1,0:T(8,128)(2,1)S(1)}, bf16[1,384,1280]{2,1,0:T(8,128)(2,1)}, u32[]{:S(2)}) copy-start(bf16[1,384,1280]{2,1,0:T(8,128)(2,1)} %param.20) | copy-start | bytes 2949124
  141.2 188.4 %copy-start.11 = (f32[1280]{0:T(1024)S(1)}, f32[1280]{0:T(1024)}, u32[]{:S(2)}) copy-start(f32[1280]{0:T(1024)} %param.32) | copy-start | bytes 15364
  296.8 32.8 %copy-start.5 = (bf16[1280,3,640]{0,2,1:T(8,128)(2,1)S(1)}, bf16[1280,3,640]{0,2,1:T(8,128)(2,1)}, u32[]{:S(2)}) copy-start(bf16[1280,3,640]{0,2,1:T(8,128)(2,1)} %copy.84) | copy-start | bytes 14745604
  345.9 4.6 %copy-start.8 = (bf16[640,1280]{1,0:T(8,128)(2,1)S(1)}, bf16[640,1280]{1,0:T(8,128)(2,1)}, u32[]{:S(2)}) copy-start(bf16[640,1280]{1,0:T(8,128)(2,1)} %param.29) | copy-start | bytes 4915204
  352.7 19.0 %copy-start.12 = (f32[1280]{0:T(1024)S(1)}, f32[1280]{0:T(1024)}, u32[]{:S(2)}) copy-start(f32[1280]{0:T(1024)} %param.33) | copy-start | bytes 15364
  352.7 74.1 %all-reduce.6.cloned.1.call-start = ((), (), s32[]{:S(2)}) async-start(), calls=%async_computation.2 | async-start | bytes 2621440 | tf_op jit(solution)/shard_map/psum | solution.py:49
  370.1 1.1 copy-start.4
  371.7 58.5 %copy-start.1 = (bf16[640,1280]{1,0:T(8,128)(2,1)S(1)}, bf16[640,1280]{1,0:T(8,128)(2,1)}, u32[]{:S(2)}) copy-start(bf16[640,1280]{1,0:T(8,128)(2,1)} %param.22) | copy-start | bytes 4915204
Sparse Core Ops, SparseCore 0:
  37.5 21.2 all-gather.7
  87.2 32.0 all-reduce.3
  132.1 164.6 all-gather.5
  352.9 14.1 all-gather.9
  394.7 32.0 all-reduce.5
